TPU v7x, 32 devices: a whole 2x2x4 slice. The times are simulated.
32 devices in a mesh: dp: 16 (over z, x, core), tm: 2 (over y).
Axes of the slice: x: 2, y: 2, z: 4, core: 2. Of those that a mesh axis runs over, the one named last changes fastest.
Arguments:
- src_mel: bfloat16 [2, 128, 640], P('tm', 'dp'), may hold values from -6 to 6
- owner: int32 [2, 128], P('tm', 'dp'), may hold values from 0 to 15, as said below
- dst_pos: int32 [2, 128], P('tm', 'dp'), may hold values from 0 to 7, as said below
- keep: int32 [2, 128], P('tm', 'dp'), may hold values 0 or 1
- cotangent: bfloat16 [16, 1024, 256], P('dp', 'tm'), may hold values from -0.125 to 0.125
- w_pre: bfloat16 [560, 512], replicated, may hold values from -0.25 to 0.25
- b_pre: float32 [512], replicated, may hold values from -3 to 3
- w_ups: bfloat16 [512, 4096], P('tm'), may hold values from -0.1875 to 0.1875
- upsample_bias: float32 [256], replicated, may hold values from -3 to 3
- w_res: bfloat16 [768, 256], replicated, may hold values from -0.21875 to 0.21875
- b_res: float32 [256], replicated, may hold values from -3 to 3
Outputs:
- section_out: bfloat16 [16, 1024, 256], P('dp', 'tm')
- grad_w_pre: float32 [560, 512], replicated
- grad_b_pre: float32 [512], replicated
- grad_w_res: float32 [768, 256], replicated
- grad_b_res: float32 [256], replicated
Inputs may be any that keep to these rules, and one draw needn't show every extreme that they name: Within one tm column, every dp index sends at most one of its segments to each owner, and every owner receives exactly 8 segments. `dst_pos`: the segments received by one owner in one column have positions 0 to 7, each once.
All inputs are finite; a program needn't handle non-finite values. No bound on the sum of `keep` on one device may be relied on, other than what follows from the above.
Results may differ from a plain program's by a relative error of at most 0.009.
The roundings to bfloat16 on the way count: a program that leaves them out, or rounds other values in their place, can miss the bound.
Values may be sent and summed in bfloat16 or wider, within the bound.
No kernel may reach another device: no remote copies, remote signals or barrier semaphores. Data moves between devices by JAX's collectives and lax.ppermute only.
A program may use at most 64 MiB of HBM per device.

v0:
```python
import jax
import jax.numpy as jnp
from jax import lax
from jax.sharding import PartitionSpec as P

KPRE = 7
UPSAMPLE_FACTOR = 8
DILATION_SIZE = 3


def with_halo(block, sides, width):
    for axis, dim in sides:
        count = lax.axis_size(axis)
        forward = [(i, i + 1) for i in range(count - 1)]
        backward = [(target, source) for source, target in forward]
        low = lax.ppermute(
            lax.slice_in_dim(block, block.shape[dim] - width, None, axis=dim), axis, forward
        )
        high = lax.ppermute(lax.slice_in_dim(block, 0, width, axis=dim), axis, backward)
        block = jnp.concatenate([low, block, high], axis=dim)
    return block


def leaky(value):
    return jnp.where(value > 0, value, 0.1 * value)


def negative_slope(value):
    return jnp.where(value > 0, 1.0, 0.1).astype(jnp.float32)


def contract_rows(left, right):
    return lax.dot_general(
        left, right, (((0,), (0,)), ((), ())), preferred_element_type=jnp.float32
    )


def contract_cols(left, right):
    return lax.dot_general(
        left, right, (((1,), (1,)), ((), ())), preferred_element_type=jnp.float32
    )


def local_pass(
    mel_ext,
    gradient_value,
    first_frame0,
    total,
    w_pre,
    b_pre,
    ups_forward,
    ups_backward,
    upsample_bias,
    w_res,
    b_res,
):
    mel_bins = mel_ext.shape[1]
    kpre = w_pre.shape[0] // mel_bins
    edge = kpre // 2 + 1
    frame_count = mel_ext.shape[0] - 2 * edge
    window_width = upsample_bias.shape[0]
    residual_kernel = w_res.shape[0] // window_width
    patches = jnp.concatenate([mel_ext[i : i + frame_count + 2] for i in range(kpre)], axis=1)
    pre = jnp.dot(patches, w_pre, preferred_element_type=jnp.float32) + b_pre
    frame_idx = first_frame0 - 1 + jnp.arange(frame_count + 2, dtype=jnp.int32)
    inside_f = ((frame_idx >= 0) & (frame_idx < total))[:, None]
    act = jnp.where(inside_f, leaky(pre), 0.0).astype(jnp.bfloat16)
    taps = ups_forward(act).reshape(frame_count + 2, 2 * UPSAMPLE_FACTOR, window_width)
    upper_output = taps[1:, :UPSAMPLE_FACTOR] + taps[:-1, UPSAMPLE_FACTOR:]
    sample_count = UPSAMPLE_FACTOR * frame_count
    start_offset = UPSAMPLE_FACTOR // 2 - DILATION_SIZE
    waveform = (
        upper_output.reshape(UPSAMPLE_FACTOR * (frame_count + 1), window_width)[
            start_offset : start_offset + sample_count + 2 * DILATION_SIZE
        ]
        + upsample_bias
    )
    step_index = (
        UPSAMPLE_FACTOR * first_frame0
        - DILATION_SIZE
        + jnp.arange(sample_count + 2 * DILATION_SIZE, dtype=jnp.int32)
    )
    inside_samples = ((step_index >= 0) & (step_index < UPSAMPLE_FACTOR * total))[:, None]
    hidden_state = jnp.where(inside_samples, leaky(waveform), 0.0).astype(jnp.bfloat16)
    column_block = jnp.concatenate(
        [
            hidden_state[kernel_index * DILATION_SIZE : kernel_index * DILATION_SIZE + sample_count]
            for kernel_index in range(residual_kernel)
        ],
        axis=1,
    )
    convolve_fn = jnp.dot(column_block, w_res, preferred_element_type=jnp.float32) + b_res
    output_rows = (waveform[DILATION_SIZE : DILATION_SIZE + sample_count] + convolve_fn).astype(
        jnp.bfloat16
    )
    g_wres = contract_rows(column_block, gradient_value)
    g_bres = jnp.sum(gradient_value.astype(jnp.float32), axis=0)
    backward_pass = contract_cols(gradient_value, w_res)
    hidden_gradient = jnp.zeros((sample_count + 2 * DILATION_SIZE, window_width), jnp.float32)
    for kernel_index in range(residual_kernel):
        hidden_gradient = hidden_gradient + jnp.pad(
            backward_pass[:, kernel_index * window_width : (kernel_index + 1) * window_width],
            (
                (
                    kernel_index * DILATION_SIZE,
                    (residual_kernel - 1 - kernel_index) * DILATION_SIZE,
                ),
                (0, 0),
            ),
        )
    waveform_gradient = jnp.where(
        inside_samples, hidden_gradient * negative_slope(waveform), 0.0
    ) + jnp.pad(gradient_value.astype(jnp.float32), ((DILATION_SIZE, DILATION_SIZE), (0, 0)))
    waveform_gradient = waveform_gradient.astype(jnp.bfloat16)
    d_upper = jnp.pad(waveform_gradient, ((start_offset, start_offset), (0, 0))).reshape(
        frame_count + 1, UPSAMPLE_FACTOR, window_width
    )
    zero_row = jnp.zeros((1, UPSAMPLE_FACTOR, window_width), jnp.bfloat16)
    d_taps = jnp.concatenate(
        [
            jnp.concatenate([zero_row, d_upper], axis=0),
            jnp.concatenate([d_upper, zero_row], axis=0),
        ],
        axis=1,
    )
    d_act = ups_backward(d_taps.reshape(frame_count + 2, 2 * UPSAMPLE_FACTOR * window_width))
    d_pre = jnp.where(inside_f, d_act * negative_slope(pre), 0.0).astype(jnp.bfloat16)
    g_wpre = contract_rows(patches, d_pre)
    g_bpre = jnp.sum(d_pre.astype(jnp.float32), axis=0)
    return (output_rows, (g_wpre, g_bpre, g_wres, g_bres))


def on_device(
    src_mel, owner, dst_pos, keep, cotangent, w_pre, b_pre, w_ups, upsample_bias, w_res, b_res
):
    owners_count = lax.axis_size("dp")
    seg_rows = src_mel[0]
    seg_count = seg_rows.shape[0]
    mel_bins = w_pre.shape[0] // KPRE
    pick = jnp.arange(owners_count, dtype=jnp.int32)[:, None] == owner[0][None, :]
    seg_width = seg_rows.shape[1]
    header = jnp.stack([dst_pos[0] + 1, keep[0]], axis=1).astype(jnp.bfloat16)
    seg_ext = jnp.concatenate([seg_rows, header], axis=1)
    outgoing = jnp.dot(
        pick.astype(jnp.bfloat16), seg_ext, preferred_element_type=jnp.float32
    ).astype(jnp.bfloat16)
    arrived = lax.all_to_all(outgoing, "dp", split_axis=0, concat_axis=0, tiled=True)
    slot_code = arrived[:, seg_width].astype(jnp.int32)
    keep_code = arrived[:, seg_width + 1].astype(jnp.int32)
    place = (slot_code - 1)[:, None] == jnp.arange(seg_count, dtype=jnp.int32)[None, :]
    mel_segs = contract_rows(place.astype(jnp.bfloat16), arrived[:, :seg_width]).astype(
        jnp.bfloat16
    )
    keep_segs = jnp.sum(jnp.where(place, keep_code[:, None], 0), axis=0)
    mel = mel_segs.reshape(seg_count * (mel_segs.shape[1] // mel_bins), mel_bins)
    frame_count = mel.shape[0]
    mel_ext = with_halo(mel, (("tm", 0),), KPRE // 2 + 1)
    first_frame0 = lax.axis_index("tm") * frame_count
    total = lax.axis_size("tm") * frame_count
    cot = cotangent[0]
    marks = jnp.repeat(keep_segs, cot.shape[0] // seg_count)
    gradient_value = jnp.where(marks[:, None] > 0, cot, jnp.zeros_like(cot))
    whole = lax.all_gather(w_ups, "tm", axis=0, tiled=True)

    def ups_forward(act):
        return jnp.dot(act, whole, preferred_element_type=jnp.float32)

    def ups_backward(d_taps):
        return contract_cols(d_taps, whole)

    output_rows, grads = local_pass(
        mel_ext,
        gradient_value,
        first_frame0,
        total,
        w_pre,
        b_pre,
        ups_forward,
        ups_backward,
        upsample_bias,
        w_res,
        b_res,
    )
    summed = lax.psum(grads, ("dp", "tm"))
    return (output_rows[None], summed[0], summed[1], summed[2], summed[3])


def solution(mesh):
    in_specs = (
        P("tm", "dp", None),
        P("tm", "dp"),
        P("tm", "dp"),
        P("tm", "dp"),
        P("dp", "tm", None),
        P(),
        P(),
        P("tm", None),
        P(),
        P(),
        P(),
    )
    out_specs = (P("dp", "tm", None), P(), P(), P(), P())
    return jax.shard_map(
        on_device, mesh=mesh, in_specs=in_specs, out_specs=out_specs, check_vma=False
    )
```

profile of v0, /device:TPU:0, one launch (start us, length us, event | category | flops | bytes accessed | tf_op | source)
XLA Modules:
  0.0 224.1 jit_solution(13383541488804429791)
XLA Ops:
  7.3 0.7 all-gather.2.cloned.1.call-update
  8.2 0.2 fusion.5
  8.4 0.5 broadcast.94
  8.9 0.7 reduce.4
  9.6 0.7 reshape.74
  10.3 7.4 %all-to-all-start = ((bf16[16,2,321]{2,1,0:T(2,128)(2,1)}), bf16[16,2,321]{2,1,0:T(2,128)(2,1)S(1)}, u32[]{:S(2)}, u32[]{:S(2)}) async-start(bf16[16,2,321]{2,1,0:T(2,128)(2,1)} %reshape.74), calls=%async_computation | async-start | bytes 49152 | tf_op jit(solution)/shard_map/all_to_all | solution.py:147
  17.7 6.5 %all-to-all-done = bf16[16,2,321]{2,1,0:T(2,128)(2,1)S(1)} async-done(((bf16[16,2,321]{2,1,0:T(2,128)(2,1)}), bf16[16,2,321]{2,1,0:T(2,128)(2,1)S(1)}, u32[]{:S(2)}, u32[]{:S(2)}) %all-to-all-start) | async-done | bytes 20576 | tf_op jit(solution)/shard_map/all_to_all | solution.py:147
  24.3 0.2 convert_reduce_fusion.2
  24.7 1.3 collective-permute-start.1
  26.3 0.1 fusion.42
  26.5 0.4 fusion.43
  27.1 4.5 %collective-permute-start = (bf16[4,80]{1,0:T(4,128)(2,1)S(1)}, bf16[4,80]{1,0:T(4,128)(2,1)S(1)}, u32[]{:S(2)}, u32[]{:S(2)}) collective-permute-start(bf16[4,80]{1,0:T(4,128)(2,1)S(1)} %get-tuple-element.27), channel_id=1, source_target_pairs={{0,1},{2,3},{4,5},{6,7},{8,9},{10,11},{12,13},{14,15},{16,17},{18,... | collective-permute-start | bytes 1928 | tf_op jit(solution)/shard_map/ppermute | solution.py:16
  31.6 1.3 collective-permute-done
  33.0 0.1 concatenate.36
  33.1 0.2 convolution_add_fusion.1
  33.4 35.7 %all-gather.2.cloned.1.call-done = bf16[512,4096]{1,0:T(8,128)(2,1)} async-done(((bf16[256,4096]{1,0:T(8,128)(2,1)}), bf16[512,4096]{1,0:T(8,128)(2,1)}) %all-gather.2.cloned.1.call-update) | async-done | bytes 4194320 | tf_op jit(solution)/shard_map/all_gather | solution.py:163
  69.1 3.1 %fusion.19 = f32[66,4096]{1,0:T(8,128)S(1)} fusion(bf16[512,4096]{1,0:T(8,128)(2,1)} %all-gather.2.cloned.1.call-done, f32[66,512]{1,0:T(8,128)S(1)} %convolution_add_fusion.1, pred[66]{0:T(512)(128)(4,1)S(1)} %compare_and_fusion), kind=kOutput, calls=%fused_computation.37 | convolution fusion | flops 276993024 | bytes 5410882 | tf_op jit(solution)/shard_map/dot_general | solution.py:166
  72.2 0.4 copy.30
  72.8 0.5 copy-done.12
  73.3 0.3 fusion.12
  73.6 0.1 fusion.14
  74.1 0.2 copy.31
  74.3 1.7 copy-done.1
  76.0 1.4 convert_reduce_fusion
  77.4 1.3 fusion.48
  78.7 1.4 fusion.16
  80.2 0.2 convert_reduce_fusion.1
  80.3 39.7 %all-reduce.7 = (f32[512]{0:T(512)}, f32[256]{0:T(256)}) all-reduce(f32[512]{0:T(512)S(1)} %get-tuple-element.28, f32[256]{0:T(256)S(1)} %convert_reduce_fusion.1), channel_id=1, replica_groups=mesh['dp'=16,'tm'=2] {'dp','tm'}, use_global_device_ids=true, to_apply=%region_3.4 | all-reduce | flops 768 | bytes 6144 | tf_op jit(solution)/shard_map/psum | solution.py:184
  120.0 1.1 fusion.2
  121.1 92.8 %all-reduce.11.cloned.1.call-done = (f32[560,512]{1,0:T(8,128)}, f32[768,256]{1,0:T(8,128)}) async-done(((f32[560,512]{1,0:T(8,128)}, f32[768,256]{1,0:T(8,128)}), (f32[560,512]{1,0:T(8,128)}, f32[768,256]{1,0:T(8,128)})) %all-reduce.11.cloned.1.call-update) | async-done | bytes 1933328 | tf_op jit(solution)/shard_map/psum | solution.py:184
  213.9 2.4 %copy.38 = f32[560,512]{1,0:T(8,128)} copy(f32[560,512]{1,0:T(8,128)} %get-tuple-element.31) | data formatting | bytes 2293760
  216.3 0.9 copy.39
  (62 shorter events, 1.6 us)
Async XLA Ops:
  7.2 25.9 %copy-start = (bf16[560,512]{1,0:T(8,128)(2,1)S(1)}, bf16[560,512]{1,0:T(8,128)(2,1)}, u32[]{:S(2)}) copy-start(bf16[560,512]{1,0:T(8,128)(2,1)} %param.16) | copy-start | bytes 1720324
  7.2 0.8 copy-start.15
  7.2 0.9 copy-start.16
  7.2 1.0 copy-start.13
  7.2 1.0 copy-start.10
  7.2 19.1 %copy-start.2 = (bf16[1,512,256]{2,1,0:T(8,128)(2,1)S(1)}, bf16[1,512,256]{2,1,0:T(8,128)(2,1)}, u32[]{:S(2)}) copy-start(bf16[1,512,256]{2,1,0:T(8,128)(2,1)} %param.15) | copy-start | bytes 786436
  7.2 19.3 %copy-start.8 = (bf16[768,256]{1,0:T(8,128)(2,1)S(1)}, bf16[768,256]{1,0:T(8,128)(2,1)}, u32[]{:S(2)}) copy-start(bf16[768,256]{1,0:T(8,128)(2,1)} %param.20) | copy-start | bytes 1179652
  7.2 61.9 %all-gather.2.cloned.1.call-start = ((), (), s32[]{:S(2)}) async-start(), calls=%async_computation.1 | async-start | bytes 6291456 | tf_op jit(solution)/shard_map/all_gather | solution.py:163
  10.3 13.9 %all-to-all-start = ((bf16[16,2,321]{2,1,0:T(2,128)(2,1)}), bf16[16,2,321]{2,1,0:T(2,128)(2,1)S(1)}, u32[]{:S(2)}, u32[]{:S(2)}) async-start(bf16[16,2,321]{2,1,0:T(2,128)(2,1)} %reshape.74), calls=%async_computation | async-start | bytes 49152 | tf_op jit(solution)/shard_map/all_to_all | solution.py:147
  17.6 196.3 %all-reduce.11.cloned.1.call-start = ((), (), s32[]{:S(2)}) async-start(), calls=%async_computation.2 | async-start | bytes 3866624 | tf_op jit(solution)/shard_map/psum | solution.py:184
  24.7 6.9 %collective-permute-start.1 = (bf16[4,80]{1,0:T(4,128)(2,1)S(1)}, bf16[4,80]{1,0:T(4,128)(2,1)S(1)}, u32[]{:S(2)}, u32[]{:S(2)}) collective-permute-start(bf16[4,80]{1,0:T(4,128)(2,1)S(1)} %get-tuple-element.26), channel_id=1, source_target_pairs={{1,0},{3,2},{5,4},{7,6},{9,8},{11,10},{13,12},{15,14},{17,16},{19,... | collective-permute-start | bytes 1928 | tf_op jit(solution)/shard_map/ppermute | solution.py:19
  26.9 6.2 %copy-start.11 = (f32[512]{0:T(512)S(1)}, f32[512]{0:T(512)}, u32[]{:S(2)}) copy-start(f32[512]{0:T(512)} %param.17) | copy-start | bytes 6148
  27.1 5.8 %collective-permute-start = (bf16[4,80]{1,0:T(4,128)(2,1)S(1)}, bf16[4,80]{1,0:T(4,128)(2,1)S(1)}, u32[]{:S(2)}, u32[]{:S(2)}) collective-permute-start(bf16[4,80]{1,0:T(4,128)(2,1)S(1)} %get-tuple-element.27), channel_id=1, source_target_pairs={{0,1},{2,3},{4,5},{6,7},{8,9},{10,11},{12,13},{14,15},{16,17},{18,... | collective-permute-start | bytes 1928 | tf_op jit(solution)/shard_map/ppermute | solution.py:16
  33.1 39.1 %copy-start.5 = (bf16[66,560]{1,0:T(8,128)(2,1)}, bf16[66,560]{1,0:T(8,128)(2,1)S(1)}, u32[]{:S(2)}) copy-start(bf16[66,560]{1,0:T(8,128)(2,1)S(1)} %concatenate.36) | copy-start | bytes 221764
  33.4 38.8 %copy-start.3 = (f32[66,512]{1,0:T(8,128)}, f32[66,512]{1,0:T(8,128)S(1)}, u32[]{:S(2)}) copy-start(f32[66,512]{1,0:T(8,128)S(1)} %convolution_add_fusion.1) | copy-start | bytes 405508
  72.6 0.7 copy-start.12
  73.8 2.2 copy-start.1
  74.0 2.0 copy-start.4
  76.0 1.4 copy-start.6
  80.1 39.9 %copy-start.9 = (bf16[768,256]{1,0:T(8,128)(2,1)S(1)}, bf16[768,256]{1,0:T(8,128)(2,1)}, u32[]{:S(2)}) copy-start(bf16[768,256]{1,0:T(8,128)(2,1)} %param.20) | copy-start | bytes 1179652
  80.1 39.9 %copy-start.14 = (f32[256]{0:T(256)S(1)}, f32[256]{0:T(256)}, u32[]{:S(2)}) copy-start(f32[256]{0:T(256)} %param.21) | copy-start | bytes 3076
  213.9 2.4 %copy-start.7 = (f32[768,256]{1,0:T(8,128)S(1)}, f32[768,256]{1,0:T(8,128)}, u32[]{:S(2)}) copy-start(f32[768,256]{1,0:T(8,128)} %get-tuple-element.33) | copy-start | bytes 2359300
Sparse Core Ops, SparseCore 0:
  9.6 59.4 all-gather.1
  80.3 133.6 all-reduce.10
where the time goes:
time: 224 us
  waiting for transfers between devices  137 us (61%)
  blocking collectives  39.7 us (18%)
  between operations  14.4 us (6%)
  starting transfers between devices  13.3 us (6%)
  matrix products  9.26 us (4%)
  local copies, waits for them, and re-layouts  8.51 us (4%)
    psum x1, waiting for transfers between devices, on_device(): summed = lax.psum(grads, ('dp', 'tm'))  92.8 us
    psum x1, blocking collectives, on_device(): summed = lax.psum(grads, ('dp', 'tm'))  39.7 us
    all_gather x1, waiting for transfers between devices, on_device(): whole = lax.all_gather(w_ups, 'tm', axis=0, tiled=True)  35.7 us
    all_to_all x1, starting transfers between devices, on_device(): lax.all_to_all(outgoing, 'dp', split_axis=0, concat_axis=0, tiled=True)  7.36 us
    unnamed x43, local copies, waits for them, and re-layouts  7 us
    all_to_all x1, waiting for transfers between devices, on_device(): lax.all_to_all(outgoing, 'dp', split_axis=0, concat_axis=0, tiled=True)  6.48 us
    ppermute x1, starting transfers between devices, with_halo(): lax.ppermute(lax.slice_in_dim(block, block.shape[dim] - width, None, axis...  4.54 us
  transfers between devices with their start and end apart: 5, of which 4 were waited for; matrix products, arithmetic and copies ran while one was open for 2% of the time, Pallas kernels for 0%

commit v1 on v0

--- a/solution.py
+++ b/solution.py
@@ -181,7 +181,8 @@
         w_res,
         b_res,
     )
-    summed = lax.psum(grads, ("dp", "tm"))
+    half = lax.psum(grads, "tm")
+    summed = lax.psum(half, "dp")
     return (output_rows[None], summed[0], summed[1], summed[2], summed[3])
 
 

time: 224 us -> 251 us (1.12)
  waiting for transfers between devices: 137 us -> 165 us
    psum x1 -> x2, waiting for transfers between devices: 92.8 us -> 121 us  [the longest x1 61.4 us: on_device(): summed = lax.psum(half, 'dp')]
    psum x1 -> x2, blocking collectives: 39.7 us -> 38.2 us  [the longest x1 33.3 us: on_device(): summed = lax.psum(half, 'dp')]
  transfers between devices with their start and end apart: 5 -> 6, of which waited for: 4 -> 5; matrix products, arithmetic and copies ran while one was open for 2% -> 2% of each run, Pallas kernels for 0% -> 0%
where the time goes in v1:
time: 251 us; the launch traced here: 250 us
  waiting for transfers between devices  165 us (66%)
  blocking collectives  38.2 us (15%)
  between operations  14.2 us (6%)
  starting transfers between devices  13.3 us (5%)
  matrix products  9.26 us (4%)
  local copies, waits for them, and re-layouts  8.47 us (3%)
    psum x1, waiting for transfers between devices, on_device(): summed = lax.psum(half, 'dp')  61.4 us
    psum x1, waiting for transfers between devices, on_device(): half = lax.psum(grads, 'tm')  59.6 us
    all_gather x1, waiting for transfers between devices, on_device(): whole = lax.all_gather(w_ups, 'tm', axis=0, tiled=True)  35.7 us
    psum x1, blocking collectives, on_device(): summed = lax.psum(half, 'dp')  33.3 us
    all_to_all x1, starting transfers between devices, on_device(): lax.all_to_all(outgoing, 'dp', split_axis=0, concat_axis=0, tiled=True)  7.36 us
    unnamed x43, local copies, waits for them, and re-layouts  6.96 us
    all_to_all x1, waiting for transfers between devices, on_device(): lax.all_to_all(outgoing, 'dp', split_axis=0, concat_axis=0, tiled=True)  6.48 us
  transfers between devices with their start and end apart: 6, of which 5 were waited for; matrix products, arithmetic and copies ran while one was open for 2% of the time, Pallas kernels for 0%

profile of v1, /device:TPU:0, one launch (start us, length us, event | category | flops | bytes accessed | tf_op | source)
XLA Modules:
  0.0 250.5 jit_solution(7799366341063224146)
XLA Ops:
  7.3 0.7 all-gather.2.cloned.1.call-update
  8.2 0.2 fusion.5
  8.4 0.5 broadcast.94
  8.9 0.7 reduce.4
  9.6 0.7 reshape.74
  10.3 7.4 %all-to-all-start = ((bf16[16,2,321]{2,1,0:T(2,128)(2,1)}), bf16[16,2,321]{2,1,0:T(2,128)(2,1)S(1)}, u32[]{:S(2)}, u32[]{:S(2)}) async-start(bf16[16,2,321]{2,1,0:T(2,128)(2,1)} %reshape.74), calls=%async_computation | async-start | bytes 49152 | tf_op jit(solution)/shard_map/all_to_all | solution.py:147
  17.7 6.5 %all-to-all-done = bf16[16,2,321]{2,1,0:T(2,128)(2,1)S(1)} async-done(((bf16[16,2,321]{2,1,0:T(2,128)(2,1)}), bf16[16,2,321]{2,1,0:T(2,128)(2,1)S(1)}, u32[]{:S(2)}, u32[]{:S(2)}) %all-to-all-start) | async-done | bytes 20576 | tf_op jit(solution)/shard_map/all_to_all | solution.py:147
  24.3 0.2 convert_reduce_fusion.2
  24.7 1.3 collective-permute-start.1
  26.3 0.1 fusion.42
  26.5 0.4 fusion.43
  27.1 4.5 %collective-permute-start = (bf16[4,80]{1,0:T(4,128)(2,1)S(1)}, bf16[4,80]{1,0:T(4,128)(2,1)S(1)}, u32[]{:S(2)}, u32[]{:S(2)}) collective-permute-start(bf16[4,80]{1,0:T(4,128)(2,1)S(1)} %get-tuple-element.31), channel_id=1, source_target_pairs={{0,1},{2,3},{4,5},{6,7},{8,9},{10,11},{12,13},{14,15},{16,17},{18,... | collective-permute-start | bytes 1928 | tf_op jit(solution)/shard_map/ppermute | solution.py:16
  31.6 1.3 collective-permute-done
  33.1 0.2 convolution_add_fusion.1
  33.4 35.7 %all-gather.2.cloned.1.call-done = bf16[512,4096]{1,0:T(8,128)(2,1)} async-done(((bf16[256,4096]{1,0:T(8,128)(2,1)}), bf16[512,4096]{1,0:T(8,128)(2,1)}) %all-gather.2.cloned.1.call-update) | async-done | bytes 4194320 | tf_op jit(solution)/shard_map/all_gather | solution.py:163
  69.1 3.1 %fusion.19 = f32[66,4096]{1,0:T(8,128)S(1)} fusion(bf16[512,4096]{1,0:T(8,128)(2,1)} %all-gather.2.cloned.1.call-done, f32[66,512]{1,0:T(8,128)S(1)} %convolution_add_fusion.1, pred[66]{0:T(512)(128)(4,1)S(1)} %compare_and_fusion), kind=kOutput, calls=%fused_computation.37 | convolution fusion | flops 276993024 | bytes 5410882 | tf_op jit(solution)/shard_map/dot_general | solution.py:166
  72.2 0.4 copy.30
  72.8 0.5 copy-done.12
  73.3 0.3 fusion.12
  73.8 0.2 copy.31
  74.3 1.6 copy-done.1
  75.9 1.4 convert_reduce_fusion
  77.3 1.3 fusion.48
  78.7 1.4 fusion.16
  80.2 59.6 %all-reduce.16.cloned.1.call-done = (f32[560,512]{1,0:T(8,128)}, f32[768,256]{1,0:T(8,128)}) async-done(((f32[560,512]{1,0:T(8,128)}, f32[768,256]{1,0:T(8,128)}), (f32[560,512]{1,0:T(8,128)}, f32[768,256]{1,0:T(8,128)})) %all-reduce.16.cloned.1.call-update) | async-done | bytes 1933328 | tf_op jit(solution)/shard_map/psum | solution.py:184
  139.8 0.2 convert_reduce_fusion.1
  140.0 4.9 %all-reduce.9 = (f32[512]{0:T(512)S(1)}, f32[256]{0:T(256)S(1)}) all-reduce(f32[512]{0:T(512)S(1)} %get-tuple-element.32, f32[256]{0:T(256)S(1)} %convert_reduce_fusion.1), channel_id=1, replica_groups=mesh['dp'=16,'tm'=2] {'tm'}, use_global_device_ids=true, to_apply=%region_4.5 | all-reduce | flops 768 | bytes 6144 | tf_op jit(solution)/shard_map/psum | solution.py:184
  144.9 33.3 %all-reduce.7 = (f32[512]{0:T(512)}, f32[256]{0:T(256)}) all-reduce(f32[512]{0:T(512)S(1)} %get-tuple-element.11, f32[256]{0:T(256)S(1)} %get-tuple-element.12), channel_id=1, replica_groups=mesh['dp'=16,'tm'=2] {'dp'}, use_global_device_ids=true, to_apply=%region_5.6 | all-reduce | flops 768 | bytes 6144 | tf_op jit(solution)/shard_map/psum | solution.py:185
  178.2 1.1 fusion.2
  179.3 61.4 %all-reduce.14.cloned.1.call-done = (f32[560,512]{1,0:T(8,128)}, f32[768,256]{1,0:T(8,128)}) async-done(((f32[560,512]{1,0:T(8,128)}, f32[768,256]{1,0:T(8,128)}), (f32[560,512]{1,0:T(8,128)}, f32[768,256]{1,0:T(8,128)})) %all-reduce.14.cloned.1.call-update) | async-done | bytes 1933328 | tf_op jit(solution)/shard_map/psum | solution.py:185
  240.6 2.4 copy.40
  243.0 0.9 copy.41
  (66 shorter events, 1.9 us)
Async XLA Ops:
  7.2 25.9 %copy-start = (bf16[560,512]{1,0:T(8,128)(2,1)S(1)}, bf16[560,512]{1,0:T(8,128)(2,1)}, u32[]{:S(2)}) copy-start(bf16[560,512]{1,0:T(8,128)(2,1)} %param.16) | copy-start | bytes 1720324
  7.2 0.8 copy-start.15
  7.2 0.9 copy-start.16
  7.2 1.0 copy-start.13
  7.2 1.0 copy-start.10
  7.2 19.1 %copy-start.2 = (bf16[1,512,256]{2,1,0:T(8,128)(2,1)S(1)}, bf16[1,512,256]{2,1,0:T(8,128)(2,1)}, u32[]{:S(2)}) copy-start(bf16[1,512,256]{2,1,0:T(8,128)(2,1)} %param.15) | copy-start | bytes 786436
  7.2 19.3 %copy-start.8 = (bf16[768,256]{1,0:T(8,128)(2,1)S(1)}, bf16[768,256]{1,0:T(8,128)(2,1)}, u32[]{:S(2)}) copy-start(bf16[768,256]{1,0:T(8,128)(2,1)} %param.20) | copy-start | bytes 1179652
  7.2 61.9 %all-gather.2.cloned.1.call-start = ((), (), s32[]{:S(2)}) async-start(), calls=%async_computation.1 | async-start | bytes 6291456 | tf_op jit(solution)/shard_map/all_gather | solution.py:163
  10.3 13.9 %all-to-all-start = ((bf16[16,2,321]{2,1,0:T(2,128)(2,1)}), bf16[16,2,321]{2,1,0:T(2,128)(2,1)S(1)}, u32[]{:S(2)}, u32[]{:S(2)}) async-start(bf16[16,2,321]{2,1,0:T(2,128)(2,1)} %reshape.74), calls=%async_computation | async-start | bytes 49152 | tf_op jit(solution)/shard_map/all_to_all | solution.py:147
  17.6 122.1 %all-reduce.16.cloned.1.call-start = ((), (), s32[]{:S(2)}) async-start(), calls=%async_computation.3 | async-start | bytes 3866624 | tf_op jit(solution)/shard_map/psum | solution.py:184
  24.7 6.9 %collective-permute-start.1 = (bf16[4,80]{1,0:T(4,128)(2,1)S(1)}, bf16[4,80]{1,0:T(4,128)(2,1)S(1)}, u32[]{:S(2)}, u32[]{:S(2)}) collective-permute-start(bf16[4,80]{1,0:T(4,128)(2,1)S(1)} %get-tuple-element.30), channel_id=1, source_target_pairs={{1,0},{3,2},{5,4},{7,6},{9,8},{11,10},{13,12},{15,14},{17,16},{19,... | collective-permute-start | bytes 1928 | tf_op jit(solution)/shard_map/ppermute | solution.py:19
  26.9 6.2 %copy-start.11 = (f32[512]{0:T(512)S(1)}, f32[512]{0:T(512)}, u32[]{:S(2)}) copy-start(f32[512]{0:T(512)} %param.17) | copy-start | bytes 6148
  27.1 5.8 %collective-permute-start = (bf16[4,80]{1,0:T(4,128)(2,1)S(1)}, bf16[4,80]{1,0:T(4,128)(2,1)S(1)}, u32[]{:S(2)}, u32[]{:S(2)}) collective-permute-start(bf16[4,80]{1,0:T(4,128)(2,1)S(1)} %get-tuple-element.31), channel_id=1, source_target_pairs={{0,1},{2,3},{4,5},{6,7},{8,9},{10,11},{12,13},{14,15},{16,17},{18,... | collective-permute-start | bytes 1928 | tf_op jit(solution)/shard_map/ppermute | solution.py:16
  33.1 39.1 %copy-start.5 = (bf16[66,560]{1,0:T(8,128)(2,1)}, bf16[66,560]{1,0:T(8,128)(2,1)S(1)}, u32[]{:S(2)}) copy-start(bf16[66,560]{1,0:T(8,128)(2,1)S(1)} %concatenate.36) | copy-start | bytes 221764
  33.4 38.8 %copy-start.3 = (f32[66,512]{1,0:T(8,128)}, f32[66,512]{1,0:T(8,128)S(1)}, u32[]{:S(2)}) copy-start(f32[66,512]{1,0:T(8,128)S(1)} %convolution_add_fusion.1) | copy-start | bytes 405508
  72.6 0.7 copy-start.12
  73.7 2.2 copy-start.1
  73.8 2.1 copy-start.4
  75.9 1.4 copy-start.6
  80.1 98.1 %copy-start.9 = (bf16[768,256]{1,0:T(8,128)(2,1)S(1)}, bf16[768,256]{1,0:T(8,128)(2,1)}, u32[]{:S(2)}) copy-start(bf16[768,256]{1,0:T(8,128)(2,1)} %param.20) | copy-start | bytes 1179652
  80.1 98.1 %copy-start.14 = (f32[256]{0:T(256)S(1)}, f32[256]{0:T(256)}, u32[]{:S(2)}) copy-start(f32[256]{0:T(256)} %param.21) | copy-start | bytes 3076
  80.1 160.5 %all-reduce.14.cloned.1.call-start = ((), (), s32[]{:S(2)}) async-start(), calls=%async_computation.2 | async-start | bytes 3866624 | tf_op jit(solution)/shard_map/psum | solution.py:185
  240.6 2.4 copy-start.7
Sparse Core Ops, SparseCore 0:
  9.6 59.4 all-gather.1
  80.2 59.5 all-reduce.15
  143.4 97.2 all-reduce.13
